TPU v7x, 512 devices: a whole 4x4x16 slice. The times are simulated.
512 devices in a mesh: walker: 32 (over z, y_lo), orb: 16 (over x, y_hi, core).
Axes of the slice: x: 4, y: 4 (y_hi: 2, y_lo: 2; y = y_hi * 2 + y_lo), z: 16, core: 2. Of those that a mesh axis runs over, the one named last changes fastest.
Arguments:
- tile_index: int32 [32768], P('walker'), may hold values from 0 to 63
- weights: bfloat16 [32768, 64], P('walker'), may hold values from -0.75 to 0.75
- electron: int32 [32768], P('walker'), may hold values from 0 to 767
- strength: float32 [32768], P('walker'), may hold values from -1.5 to 1.5
- spline_table: bfloat16 [4096, 4096], P(None, 'orb'), may hold values from -6 to 6
- rotation: bfloat16 [4096, 768], P('orb'), may hold values from -0.09375 to 0.09375
- inverse: bfloat16 [32, 768, 768], P('walker', 'orb'), may hold values from -0.21875 to 0.21875
Outputs:
- ratios: float32 [32768], P(('walker', 'orb'))
- gradient: float32 [4096, 768], P('orb')
All inputs are finite; a program needn't handle non-finite values.
Results may differ from a plain program's by a relative error of at most 0.0042.
Values may be sent and summed in bfloat16 or wider, within the bound.
No kernel may reach another device: no remote copies, remote signals or barrier semaphores. Data moves between devices by JAX's collectives and lax.ppermute only.
A program may use at most 64 MiB of HBM per device.

v0:
```python
import jax
import jax.numpy as jnp
from jax import lax
from jax.sharding import PartitionSpec as P


def body(tile_index, weights, electron, strength, spline_table, rotation, inverse):
    points = tile_index.shape[0]
    coeffs = weights.shape[1]
    tiles_count = spline_table.shape[0] // coeffs
    shards = lax.axis_size("orb")
    own_rows = points // shards
    first_point = lax.axis_index("orb") * own_rows
    onehot = (tile_index[:, None] == jnp.arange(tiles_count, dtype=jnp.int32)[None, :]).astype(
        jnp.bfloat16
    )
    stencil_matrix = (onehot[:, :, None] * weights[:, None, :]).reshape(
        points, tiles_count * coeffs
    )
    orbital_values = jnp.dot(
        stencil_matrix, spline_table, preferred_element_type=jnp.float32
    ).astype(jnp.bfloat16)
    local_inverse = inverse[0]
    rotated = lax.psum_scatter(
        lax.dot_general(
            rotation, orbital_values, (((0,), (1,)), ((), ())), preferred_element_type=jnp.float32
        ),
        "orb",
        scatter_dimension=0,
        tiled=True,
    )
    columns = jnp.take(local_inverse, electron, axis=1).astype(jnp.float32)
    partial_ratio = jnp.sum(rotated * columns, axis=0)
    ratio_total = lax.psum(partial_ratio, "orb")
    ratios = lax.dynamic_slice_in_dim(ratio_total, first_point, own_rows, 0)
    adjoint = (columns * strength[None, :]).astype(jnp.bfloat16)
    local_gradient = lax.dot_general(
        orbital_values,
        lax.all_gather(adjoint, "orb", axis=0, tiled=True),
        (((0,), (1,)), ((), ())),
        preferred_element_type=jnp.float32,
    )
    gradient = lax.psum(local_gradient, "walker")
    return (ratios, gradient)


def solution(mesh):
    in_specs = (
        P("walker"),
        P("walker", None),
        P("walker"),
        P("walker"),
        P(None, "orb"),
        P("orb", None),
        P("walker", "orb", None),
    )
    out_specs = (P(("walker", "orb")), P("orb", None))
    return jax.shard_map(body, mesh=mesh, in_specs=in_specs, out_specs=out_specs, check_vma=False)
```

profile of v0, /device:TPU:4, one launch (start us, length us, event | category | flops | bytes accessed | tf_op | source)
XLA Modules:
  0.0 463.4 jit_solution(13601765400764669437)
XLA Ops:
  7.2 0.0 copy-start
  7.2 0.0 reduce-scatter.4.cloned.1.call-start
  7.2 0.9 fusion
  8.1 1.5 broadcast_multiply_fusion
  9.5 0.0 copy-done
  9.5 0.0 copy-start.1
  9.6 2.5 convolution_convert_fusion
  12.0 0.0 copy-done.1
  12.0 2.2 convolution_bitcast_fusion
  14.3 3.5 copy.17
  17.8 0.0 copy-start.2
  17.8 0.0 copy-start.3
  17.8 0.0 copy-start.4
  17.8 0.0 reduce-scatter.4.cloned.1.call-update
  17.8 0.0 all-gather.2.cloned.1.call-start
  17.9 0.8 copy-done.2
  18.7 0.2 copy.14
  18.8 0.0 copy-done.3
  18.9 3.2 gather_fusion
  22.1 0.1 copy.15
  22.2 97.2 %reduce-scatter.4.cloned.1.call-done = f32[48,1024]{1,0:T(8,128)} async-done(((f32[768,1024]{1,0:T(8,128)}), f32[48,1024]{1,0:T(8,128)}) %reduce-scatter.4.cloned.1.call-update) | async-done | bytes 196624 | tf_op jit(solution)/shard_map/reduce_scatter | solution.py:24
  119.4 0.0 copy-done.4
  119.4 1.6 fusion.2
  121.0 0.0 all-gather.2.cloned.1.call-update
  121.0 0.0 all-reduce.2.cloned.1.call-start
  121.1 62.9 %all-gather.2.cloned.1.call-done = bf16[768,1024]{1,0:T(8,128)(2,1)} async-done(((bf16[48,1024]{1,0:T(8,128)(2,1)}), bf16[768,1024]{1,0:T(8,128)(2,1)}) %all-gather.2.cloned.1.call-update) | async-done | bytes 1572880 | tf_op jit(solution)/shard_map/all_gather | solution.py:39
  184.0 2.9 fusion.4
  186.9 0.0 all-reduce.2.cloned.1.call-update
  187.0 30.3 %psum.14 = f32[1024]{0:T(1024)S(1)} all-reduce(f32[1024]{0:T(1024)S(1)} %get-tuple-element.3), channel_id=1, replica_groups=mesh['walker'=32,'orb'=16] {'orb'}, use_global_device_ids=true, to_apply=%region_2.3 | all-reduce | flops 1024 | bytes 8192 | tf_op jit(solution)/shard_map/psum | solution.py:34
  217.3 0.6 dynamic_slice.3
  217.8 237.0 %all-reduce.2.cloned.1.call-done = f32[256,768]{1,0:T(8,128)} async-done(((f32[256,768]{1,0:T(8,128)}), f32[256,768]{1,0:T(8,128)}) %all-reduce.2.cloned.1.call-update) | async-done | bytes 786448 | tf_op jit(solution)/shard_map/psum | solution.py:43
  454.8 2.1 copy.20
  (2 shorter events, 0.0 us)
Async XLA Ops:
  7.2 2.4 copy-start
  7.2 112.2 %reduce-scatter.4.cloned.1.call-start = ((), (), s32[]{:S(2)}) async-start(), calls=%async_computation.3 | async-start | bytes 3342336 | tf_op jit(solution)/shard_map/reduce_scatter | solution.py:24
  9.5 2.5 copy-start.1
  17.8 0.9 copy-start.2
  17.8 1.1 copy-start.3
  17.8 101.6 %copy-start.4 = (f32[1024]{0:T(1024)S(1)}, f32[1024]{0:T(1024)}, u32[]{:S(2)}) copy-start(f32[1024]{0:T(1024)} %param.10) | copy-start | bytes 12292
  17.8 166.2 %all-gather.2.cloned.1.call-start = ((), (), s32[]{:S(2)}) async-start(), calls=%async_computation.1 | async-start | bytes 1671168 | tf_op jit(solution)/shard_map/all_gather | solution.py:39
  121.0 333.8 %all-reduce.2.cloned.1.call-start = ((), (), s32[]{:S(2)}) async-start(), calls=%async_computation.2 | async-start | bytes 1572864 | tf_op jit(solution)/shard_map/psum | solution.py:43
Sparse Core Ops, SparseCore 0:
  17.9 101.4 reduce-scatter.3
  123.2 60.7 all-gather.1
  187.5 267.2 all-reduce.1
where the time goes:
time: 464 us; the launch traced here: 463 us
  waiting for transfers between devices  397 us (86%)
  blocking collectives  30.3 us (7%)
  between operations  13.8 us (3%)
  local copies, waits for them, and re-layouts  10.5 us (2%)
  matrix products  7.59 us (2%)
    psum x1, waiting for transfers between devices, body(): gradient = lax.psum(local_gradient, 'walker')  237 us
    reduce_scatter x1, waiting for transfers between devices, body(): lax.psum_scatter(lax.dot_general(rotation, orbital_values, (((0,), (1,)),...  97.2 us
    all_gather x1, waiting for transfers between devices, body(): lax.all_gather(adjoint, 'orb', axis=0, tiled=True)  62.9 us
    psum x1, blocking collectives, body(): ratio_total = lax.psum(partial_ratio, 'orb')  30.3 us
  transfers between devices with their start and end apart: 3, of which 3 were waited for; matrix products, arithmetic and copies ran while one was open for 1% of the time, Pallas kernels for 0%

commit v1 on v0

--- a/solution.py
+++ b/solution.py
@@ -2,6 +2,7 @@
 import jax.numpy as jnp
 from jax import lax
 from jax.sharding import PartitionSpec as P
+from jax.lax import all_to_all, axis_size
 
 
 def body(tile_index, weights, electron, strength, spline_table, rotation, inverse):
@@ -34,9 +35,15 @@
     ratio_total = lax.psum(partial_ratio, "orb")
     ratios = lax.dynamic_slice_in_dim(ratio_total, first_point, own_rows, 0)
     adjoint = (columns * strength[None, :]).astype(jnp.bfloat16)
+
+    def proceed_positions(matrix):
+        piece_now = jnp.stack([matrix] * axis_size("orb"), 0)
+        val2 = all_to_all(piece_now, "orb", 0, 0)
+        return jnp.concatenate(val2, 0)
+
     local_gradient = lax.dot_general(
         orbital_values,
-        lax.all_gather(adjoint, "orb", axis=0, tiled=True),
+        proceed_positions(adjoint),
         (((0,), (1,)), ((), ())),
         preferred_element_type=jnp.float32,
     )

time: 464 us -> 424 us (0.914)
  waiting for transfers between devices: 397 us -> 333 us
  blocking collectives: 30.3 us -> 56.3 us
    all_gather x1 -> x0, waiting for transfers between devices: 62.9 us -> none  [body(): lax.all_gather(adjoint, 'orb', axis=0, tiled=True)]
    all_to_all x0 -> x1, blocking collectives: none -> 27.2 us  [proceed_positions(): val2 = all_to_all(piece_now, 'orb', 0, 0)]
  transfers between devices with their start and end apart: 3 -> 2, of which waited for: 3 -> 2; matrix products, arithmetic and copies ran while one was open for 1% -> 1% of each run, Pallas kernels for 0% -> 0%
where the time goes in v1:
time: 424 us
  waiting for transfers between devices  333 us (79%)
  blocking collectives  56.3 us (13%)
  between operations  14.1 us (3%)
  local copies, waits for them, and re-layouts  10.7 us (3%)
  matrix products  6.22 us (1%)
    psum x1, waiting for transfers between devices, body(): gradient = lax.psum(local_gradient, 'walker')  236 us
    reduce_scatter x1, waiting for transfers between devices, body(): lax.psum_scatter(lax.dot_general(rotation, orbital_values, (((0,), (1,)),...  97.2 us
    psum x1, blocking collectives, body(): ratio_total = lax.psum(partial_ratio, 'orb')  29.1 us
    all_to_all x1, blocking collectives, proceed_positions(): val2 = all_to_all(piece_now, 'orb', 0, 0)  27.2 us
  transfers between devices with their start and end apart: 2, of which 2 were waited for; matrix products, arithmetic and copies ran while one was open for 1% of the time, Pallas kernels for 0%

profile of v1, /device:TPU:4, one launch (start us, length us, event | category | flops | bytes accessed | tf_op | source)
XLA Modules:
  0.0 424.0 jit_solution(13199036812561367098)
XLA Ops:
  7.2 0.0 copy-start
  7.2 0.0 reduce-scatter.4.cloned.1.call-start
  7.2 0.9 fusion
  8.1 1.5 broadcast_multiply_fusion
  9.5 0.0 copy-done
  9.6 0.0 copy-start.1
  9.6 2.5 convolution_convert_fusion
  12.0 0.0 copy-done.1
  12.0 2.3 convolution_bitcast_fusion
  14.3 3.5 copy.19
  17.8 0.0 copy-start.2
  17.8 0.0 copy-start.3
  17.9 0.0 copy-start.4
  17.9 0.0 reduce-scatter.4.cloned.1.call-update
  17.9 0.0 all-reduce.2.cloned.1.call-start
  17.9 0.8 copy-done.2
  18.7 0.2 copy.16
  18.9 0.0 copy-done.3
  18.9 3.2 gather_fusion
  22.1 0.1 copy.17
  22.3 97.2 %reduce-scatter.4.cloned.1.call-done = f32[48,1024]{1,0:T(8,128)} async-done(((f32[768,1024]{1,0:T(8,128)}), f32[48,1024]{1,0:T(8,128)}) %reduce-scatter.4.cloned.1.call-update) | async-done | bytes 196624 | tf_op jit(solution)/shard_map/reduce_scatter | solution.py:25
  119.5 0.0 copy-done.4
  119.5 1.0 fusion.2
  120.4 0.2 stack.2
  120.6 27.2 %all_to_all.5 = bf16[16,48,1024]{2,1,0:T(8,128)(2,1)S(1)} all-to-all(bf16[16,48,1024]{2,1,0:T(8,128)(2,1)S(1)} %stack.2), channel_id=1, replica_groups=mesh['walker'=32,'orb'=16] {'orb'}, dimensions={0} | all-to-all | bytes 3145728 | tf_op jit(solution)/shard_map/all_to_all | solution.py:41
  147.8 1.5 fusion.4
  149.3 0.0 all-reduce.2.cloned.1.call-update
  149.3 29.1 %psum.14 = f32[1024]{0:T(1024)S(1)} all-reduce(f32[1024]{0:T(1024)S(1)} %get-tuple-element.3), channel_id=1, replica_groups=mesh['walker'=32,'orb'=16] {'orb'}, use_global_device_ids=true, to_apply=%region_2.3 | all-reduce | flops 1024 | bytes 8192 | tf_op jit(solution)/shard_map/psum | solution.py:35
  178.5 0.6 dynamic_slice.3
  179.0 236.0 %all-reduce.2.cloned.1.call-done = f32[256,768]{1,0:T(8,128)} async-done(((f32[256,768]{1,0:T(8,128)}), f32[256,768]{1,0:T(8,128)}) %all-reduce.2.cloned.1.call-update) | async-done | bytes 786448 | tf_op jit(solution)/shard_map/psum | solution.py:50
  415.1 2.1 copy.22
  (2 shorter events, 0.0 us)
Async XLA Ops:
  7.2 2.4 copy-start
  7.2 112.3 %reduce-scatter.4.cloned.1.call-start = ((), (), s32[]{:S(2)}) async-start(), calls=%async_computation.3 | async-start | bytes 3342336 | tf_op jit(solution)/shard_map/reduce_scatter | solution.py:25
  9.6 2.5 copy-start.1
  17.8 0.9 copy-start.2
  17.8 1.1 copy-start.3
  17.9 101.6 %copy-start.4 = (f32[1024]{0:T(1024)S(1)}, f32[1024]{0:T(1024)}, u32[]{:S(2)}) copy-start(f32[1024]{0:T(1024)} %param.10) | copy-start | bytes 12292
  17.9 397.2 %all-reduce.2.cloned.1.call-start = ((), (), s32[]{:S(2)}) async-start(), calls=%async_computation.2 | async-start | bytes 1572864 | tf_op jit(solution)/shard_map/psum | solution.py:50
Sparse Core Ops, SparseCore 0:
  18.0 101.4 reduce-scatter.3
  149.4 265.5 all-reduce.1
